TPU v7x, 32 devices: a whole 2x2x4 slice. The times are simulated.
32 devices in a mesh: rep: 4 (over z), tp: 8 (over y, x, core).
Axes of the slice: x: 2, y: 2, z: 4, core: 2. Of those that a mesh axis runs over, the one named last changes fastest.
Arguments:
- activations: bfloat16 [6144, 1024], P(('rep', 'tp')), may hold values from -6 to 6
- out_grads: bfloat16 [6144, 3072], P('rep', 'tp'), may hold values from -0.15625 to 0.15625
- error_state: bfloat16 [4, 1024, 3072], P('rep', None, 'tp'), may hold values from -4 to 4
- q_start: float32 [3072, 32], P('tp'), may hold values from -6 to 6
- qkv_master: float32 [1024, 3072], P('rep', 'tp'), may hold values from -3 to 3
- qkv_moment: float32 [1024, 3072], P('rep', 'tp'), may hold values from -0.75 to 0.75
- word_grads: bfloat16 [6144, 1024], P('rep', 'tp'), may hold values from -6 to 6
- token_ids: int32 [6144], P('rep'), may hold values from 0 to 1599, as said below
- owner_map: int32 [1600], replicated, may hold values from 0 to 1599, as said below
- word_master: float32 [1600, 1024], P('rep', 'tp'), may hold values from -6 to 6
Outputs:
- error_new: bfloat16 [4, 1024, 3072], P('rep', None, 'tp')
- q_factor: float32 [3072, 32], P('tp')
- moment_new: float32 [1024, 3072], P('rep', 'tp')
- master_new: float32 [1024, 3072], P('rep', 'tp')
- weight_bf16: bfloat16 [1024, 3072], P(None, 'tp')
- word_new: float32 [1600, 1024], P('rep', 'tp')
Inputs may be any that keep to these rules, and one draw needn't show every extreme that they name: A permutation of the rows: word w is stored in row owner_map[w] of word_master, whose owner is that row divided by 400. `token_ids`: the 1536 tokens of one replica name words of one owner at most 768 times; in every replica some owner is named exactly 768 times.
All inputs are finite; a program needn't handle non-finite values.
Results may differ from a plain program's by a relative error of at most 0.001.
Values may be sent and summed in bfloat16 or wider, within the bound.
No kernel may reach another device: no remote copies, remote signals or barrier semaphores. Data moves between devices by JAX's collectives and lax.ppermute only.
A program may use at most 64 MiB of HBM per device.

v0:
```python
import jax
import jax.numpy as jnp
from jax import lax
from jax.sharding import PartitionSpec as P

ROUNDS = 2
MOMENTUM = 0.9
LEARNING_RATE = 4.0
EMBED_RATE = 0.5


def orthonormal(left_basis, gram_matrix):
    factor_low = jnp.linalg.cholesky(gram_matrix)
    return jax.scipy.linalg.solve_triangular(factor_low, left_basis.T, lower=True).T


def word_update(word_grads, token_ids, owner_map, word_master):
    replicas = lax.axis_size("rep")
    per_owner = word_master.shape[0]
    capacity = 2 * token_ids.shape[0] // replicas
    targets = owner_map[token_ids]
    owners = targets // per_owner
    row_slot = targets % per_owner
    matches = (owners[:, None] == jnp.arange(replicas, dtype=jnp.int32)[None, :]).astype(jnp.int32)
    places = jnp.sum(jnp.cumsum(matches, axis=0) * matches, axis=1) - 1
    outgoing = (
        jnp.zeros((replicas, capacity, word_grads.shape[1]), jnp.bfloat16)
        .at[owners, places]
        .set(word_grads)
    )
    labels = jnp.full((replicas, capacity), per_owner, jnp.int32).at[owners, places].set(row_slot)
    incoming, arrived = (
        lax.all_to_all(outgoing, "rep", split_axis=0, concat_axis=0, tiled=True),
        lax.all_to_all(labels, "rep", split_axis=0, concat_axis=0, tiled=True),
    )
    flat_rows = incoming.reshape(-1, incoming.shape[2])
    selector = (
        arrived.reshape(-1)[:, None] == jnp.arange(per_owner, dtype=jnp.int32)[None, :]
    ).astype(jnp.bfloat16)
    row_grad = lax.dot_general(
        selector, flat_rows, (((0,), (0,)), ((), ())), preferred_element_type=jnp.float32
    )
    return word_master - EMBED_RATE * row_grad


def shards(
    activations,
    out_grads,
    error_state,
    q_start,
    qkv_master,
    qkv_moment,
    word_grads,
    token_ids,
    owner_map,
    word_master,
):
    highest = lax.Precision.HIGHEST
    replicas = lax.axis_size("rep")
    word_new = None
    product = lax.dot_general(
        lax.all_gather(activations, "tp", axis=0, tiled=True),
        out_grads,
        (((0,), (0,)), ((), ())),
        preferred_element_type=jnp.float32,
    )
    combined = product + error_state[0].astype(jnp.float32)
    right_basis = q_start
    left_basis = None
    for round_index in range(ROUNDS):
        partial_left = jnp.dot(combined, right_basis, precision=highest)
        left_basis = lax.psum(partial_left, ("rep", "tp")) / replicas
        gram_matrix = jnp.dot(left_basis.T, left_basis, precision=highest)
        left_basis = orthonormal(left_basis, gram_matrix)
        partial_right = lax.dot_general(
            combined, left_basis, (((0,), (0,)), ((), ())), precision=highest
        )
        right_basis = lax.psum(partial_right, "rep") / replicas
    approx = jnp.dot(left_basis, right_basis.T, precision=highest)
    error_new = (combined - approx).astype(jnp.bfloat16)[None]
    owned_rows = qkv_master.shape[0]
    update_rows = lax.dynamic_slice_in_dim(
        approx, lax.axis_index("rep") * owned_rows, owned_rows, 0
    )
    moment_new = MOMENTUM * qkv_moment + update_rows
    master_new = qkv_master - LEARNING_RATE * moment_new
    weight_bf16 = lax.all_gather(master_new.astype(jnp.bfloat16), "rep", axis=0, tiled=True)
    word_new = word_update(word_grads, token_ids, owner_map, word_master)
    return (error_new, right_basis, moment_new, master_new, weight_bf16, word_new)


def solution(mesh):
    in_specs = (
        P(("rep", "tp"), None),
        P("rep", "tp"),
        P("rep", None, "tp"),
        P("tp", None),
        P("rep", "tp"),
        P("rep", "tp"),
        P("rep", "tp"),
        P("rep"),
        P(),
        P("rep", "tp"),
    )
    out_specs = (
        P("rep", None, "tp"),
        P("tp", None),
        P("rep", "tp"),
        P("rep", "tp"),
        P(None, "tp"),
        P("rep", "tp"),
    )
    return jax.shard_map(shards, mesh=mesh, in_specs=in_specs, out_specs=out_specs, check_vma=False)
```

profile of v0, /device:TPU:0, one launch (start us, length us, event | category | flops | bytes accessed | tf_op | source)
XLA Modules:
  0.0 393.2 jit_solution(7987979019762832987)
XLA Ops:
  8.0 0.7 compare_select_fusion.2
  8.7 8.4 %gather_fusion = s32[1536]{0:T(1024)S(1)} fusion(s32[1600]{0:T(1024)S(1)} %copy-done.1, s32[2048]{0:T(1024)S(1)} %pad_clamp_fusion), kind=kCustom, calls=%fused_computation | custom fusion | bytes 18432 | tf_op jit(solution)/shard_map/gather | solution.py:21
  17.2 1.2 reduce-window.6
  19.1 25.9 %all-gather.2.cloned.1.call-done = bf16[1536,1024]{1,0:T(8,128)(2,1)} async-done(((bf16[192,1024]{1,0:T(8,128)(2,1)}), bf16[1536,1024]{1,0:T(8,128)(2,1)}) %all-gather.2.cloned.1.call-update) | async-done | bytes 3145744 | tf_op jit(solution)/shard_map/all_gather | solution.py:62
  45.0 3.9 convert_add_fusion
  48.9 2.2 fusion.45
  51.2 6.8 %scatter_custom_fusion = s32[3072]{0:T(1024)} fusion(s32[1536]{0:T(1024)S(1)} %broadcast_select_fusion, s32[1536]{0:T(1024)S(1)} %get-tuple-element.13, s32[]{:T(128)} %constant.83.clone.1), kind=kCustom, calls=%fused_computation.70 | custom fusion | bytes 12292
  57.9 4.6 %all-to-all-start = ((s32[4,1,768]{2,1,0:T(1,128)}), s32[4,1,768]{2,1,0:T(1,128)S(1)}, u32[]{:S(2)}, u32[]{:S(2)}) async-start(s32[4,1,768]{2,1,0:T(1,128)} %bitcast.13), calls=%async_computation | async-start | bytes 24576 | tf_op jit(solution)/shard_map/all_to_all | solution.py:34
  62.5 5.7 %scatter_custom_fusion.1 = bf16[3072,128]{1,0:T(8,128)(2,1)} fusion(s32[1536]{0:T(1024)S(1)} %broadcast_select_fusion, bf16[1536,128]{1,0:T(8,128)(2,1)} %param.19, bf16[]{:T(256)} %constant.89.clone.1), kind=kCustom, calls=%fused_computation.11 | custom fusion | bytes 786944
  68.3 105.5 %all-reduce.3.cloned.1.call-done = f32[1024,32]{0,1:T(8,128)} async-done(((f32[1024,32]{0,1:T(8,128)}), f32[1024,32]{0,1:T(8,128)}) %all-reduce.3.cloned.1.call-update) | async-done | bytes 131088 | tf_op jit(solution)/shard_map/psum | solution.py:72
  173.8 1.2 fusion.15
  175.1 2.9 cholesky.44
  178.6 3.6 all-to-all-start.1
  182.9 1.3 fusion.27
  184.1 3.2 custom-call.6
  187.3 1.2 fusion.9
  188.5 1.6 fusion.46
  190.1 21.4 %psum.29 = f32[384,32]{0,1:T(8,128)} all-reduce(f32[384,32]{0,1:T(8,128)} %fusion.46), channel_id=1, replica_groups=mesh['rep'=4,'tp'=8] {'rep'}, use_global_device_ids=true, to_apply=%region_3.0 | all-reduce | flops 12288 | bytes 98304 | tf_op jit(solution)/shard_map/psum | solution.py:78
  211.5 3.0 fusion.21
  214.6 2.5 fusion.3
  217.1 119.1 %all-reduce.5.cloned.1.call-done = f32[1024,32]{0,1:T(8,128)} async-done(((f32[1024,32]{0,1:T(8,128)}), f32[1024,32]{0,1:T(8,128)}) %all-reduce.5.cloned.1.call-update) | async-done | bytes 131088 | tf_op jit(solution)/shard_map/psum | solution.py:72
  336.1 1.2 fusion.12
  337.4 2.9 cholesky.55
  341.7 2.4 custom-call.7
  344.1 1.2 fusion.7
  345.4 1.0 fusion.47
  346.4 18.4 %psum.31 = f32[384,32]{0,1:T(8,128)S(1)} all-reduce(f32[384,32]{0,1:T(8,128)S(1)} %fusion.47), channel_id=1, replica_groups=mesh['rep'=4,'tp'=8] {'rep'}, use_global_device_ids=true, to_apply=%region_5.8 | all-reduce | flops 12288 | bytes 98304 | tf_op jit(solution)/shard_map/psum | solution.py:78
  364.8 1.5 fusion.48
  366.3 1.1 fusion.4
  367.4 1.0 fusion.44
  368.4 17.4 %all_gather.7 = bf16[1024,384]{1,0:T(8,128)(2,1)S(1)} all-gather(bf16[256,384]{1,0:T(8,128)(2,1)S(1)} %get-tuple-element.10), channel_id=1, replica_groups=mesh['rep'=4,'tp'=8] {'rep'}, dimensions={0}, use_global_device_ids=true | all-gather | bytes 983040 | tf_op jit(solution)/shard_map/all_gather | solution.py:87
  385.8 0.9 copy.27
  (51 shorter events, 4.4 us)
Async XLA Ops:
  7.2 37.8 %copy-start = (bf16[1536,384]{1,0:T(8,128)(2,1)S(1)}, bf16[1536,384]{1,0:T(8,128)(2,1)}, u32[]{:S(2)}) copy-start(bf16[1536,384]{1,0:T(8,128)(2,1)} %param.14) | copy-start | bytes 3538948
  7.2 1.5 copy-start.1
  7.2 37.8 %all-gather.2.cloned.1.call-start = ((), (), s32[]{:S(2)}) async-start(), calls=%async_computation.2 | async-start | bytes 3538944 | tf_op jit(solution)/shard_map/all_gather | solution.py:62
  7.9 165.8 %all-reduce.3.cloned.1.call-start = ((), (), s32[]{:S(2)}) async-start(), calls=%async_computation.3 | async-start | bytes 262144 | tf_op jit(solution)/shard_map/psum | solution.py:72
  8.7 10.2 %copy-start.9 = (s32[2]{0:T(128)S(1)}, s32[2]{0:T(128)}, u32[]{:S(2)}) copy-start(s32[2]{0:T(128)} %constant.92) | copy-start | bytes 28
  8.7 10.3 %copy-start.8 = (s32[2]{0:T(128)S(1)}, s32[2]{0:T(128)}, u32[]{:S(2)}) copy-start(s32[2]{0:T(128)} %constant.95) | copy-start | bytes 28
  19.1 29.8 %copy-start.5 = (f32[384,32]{0,1:T(8,128)S(1)}, f32[384,32]{0,1:T(8,128)}, u32[]{:S(2)}) copy-start(f32[384,32]{0,1:T(8,128)} %param.16) | copy-start | bytes 147460
  57.9 120.1 %all-to-all-start = ((s32[4,1,768]{2,1,0:T(1,128)}), s32[4,1,768]{2,1,0:T(1,128)S(1)}, u32[]{:S(2)}, u32[]{:S(2)}) async-start(s32[4,1,768]{2,1,0:T(1,128)} %bitcast.13), calls=%async_computation | async-start | bytes 24576 | tf_op jit(solution)/shard_map/all_to_all | solution.py:34
  178.0 0.6 copy-start.6
  178.6 35.9 %all-to-all-start.1 = ((bf16[4,768,128]{2,1,0:T(8,128)(2,1)}), bf16[4,768,128]{2,1,0:T(8,128)(2,1)S(1)}, u32[]{:S(2)}, u32[]{:S(2)}) async-start(bf16[4,768,128]{2,1,0:T(8,128)(2,1)} %bitcast.15), calls=%async_computation.1 | async-start | bytes 1572864 | tf_op jit(solution)/shard_map/all_to_all | solution.py:33
  182.2 153.9 %all-reduce.5.cloned.1.call-start = ((), (), s32[]{:S(2)}) async-start(), calls=%async_computation.4 | async-start | bytes 262144 | tf_op jit(solution)/shard_map/psum | solution.py:72
  188.5 26.1 %copy-start.7 = (s32[4,1,768]{2,1,0:T(1,128)S(1)}, s32[4,1,768]{2,1,0:T(1,128)}, u32[]{:S(2)}) copy-start(s32[4,1,768]{2,1,0:T(1,128)} %copy-done.6) | copy-start | bytes 36868
  364.8 2.6 copy-start.4
  366.3 1.2 copy-start.2
  366.3 1.2 copy-start.3
Sparse Core Ops, SparseCore 0:
  9.9 35.0 all-gather.1
  51.3 122.4 all-reduce.2
  214.7 121.4 all-reduce.4
where the time goes:
time: 394 us; the launch traced here: 393 us
  waiting for transfers between devices  251 us (64%)
  blocking collectives  57.2 us (15%)
  local copies, waits for them, and re-layouts  22.8 us (6%)
  matrix products  20.6 us (5%)
  other arithmetic  19.2 us (5%)
  between operations  14 us (4%)
  starting transfers between devices  8.25 us (2%)
    psum x2, waiting for transfers between devices, shards(): left_basis = lax.psum(partial_left, ('rep', 'tp')) / replicas  225 us
    psum x2, blocking collectives, shards(): right_basis = lax.psum(partial_right, 'rep') / replicas  39.8 us
    all_gather x1, waiting for transfers between devices, shards(): lax.all_gather(activations, 'tp', axis=0, tiled=True)  25.9 us
    all_gather x1, blocking collectives, shards(): lax.all_gather(master_new.astype(jnp.bfloat16), 'rep', axis=0, tiled=True)  17.4 us
    unnamed x23, local copies, waits for them, and re-layouts  14 us
    gather x1, local copies, waits for them, and re-layouts, word_update(): targets = owner_map[token_ids]  8.39 us
  transfers between devices with their start and end apart: 5, of which 3 were waited for; matrix products, arithmetic and copies ran while one was open for 10% of the time, Pallas kernels for 0%

commit v1 on v0

--- a/solution.py
+++ b/solution.py
@@ -69,7 +69,7 @@
     left_basis = None
     for round_index in range(ROUNDS):
         partial_left = jnp.dot(combined, right_basis, precision=highest)
-        left_basis = lax.psum(partial_left, ("rep", "tp")) / replicas
+        left_basis = lax.psum(lax.psum(partial_left, "tp"), "rep") / replicas
         gram_matrix = jnp.dot(left_basis.T, left_basis, precision=highest)
         left_basis = orthonormal(left_basis, gram_matrix)
         partial_right = lax.dot_general(

time: 394 us -> 327 us (0.83)
  waiting for transfers between devices: 251 us -> 183 us
    psum x2 -> x4, waiting for transfers between devices: 225 us -> 157 us  [shards(): left_basis = lax.psum(lax.psum(partial_left, 'tp'), 'rep') / replicas]
  transfers between devices with their start and end apart: 5 -> 7, of which waited for: 3 -> 5; matrix products, arithmetic and copies ran while one was open for 10% -> 13% of each run, Pallas kernels for 0% -> 0%
where the time goes in v1:
time: 327 us; the launch traced here: 326 us
  waiting for transfers between devices  183 us (56%)
  blocking collectives  56.7 us (17%)
  local copies, waits for them, and re-layouts  22.8 us (7%)
  matrix products  20.6 us (6%)
  other arithmetic  20.4 us (6%)
  between operations  14.1 us (4%)
  starting transfers between devices  8.48 us (3%)
    psum x4, waiting for transfers between devices, shards(): left_basis = lax.psum(lax.psum(partial_left, 'tp'), 'rep') / replicas  157 us
    psum x2, blocking collectives, shards(): right_basis = lax.psum(partial_right, 'rep') / replicas  39.2 us
    all_gather x1, waiting for transfers between devices, shards(): lax.all_gather(activations, 'tp', axis=0, tiled=True)  26 us
    all_gather x1, blocking collectives, shards(): lax.all_gather(master_new.astype(jnp.bfloat16), 'rep', axis=0, tiled=True)  17.5 us
    unnamed x23, local copies, waits for them, and re-layouts  14 us
    gather x1, local copies, waits for them, and re-layouts, word_update(): targets = owner_map[token_ids]  8.39 us
    another operation x6, other arithmetic, orthonormal(): factor_low = jnp.linalg.cholesky(gram_matrix)  8.37 us
    another operation x4, other arithmetic, orthonormal(): jax.scipy.linalg.solve_triangular(factor_low, left_basis.T, lower=True)  7.49 us
  transfers between devices with their start and end apart: 7, of which 5 were waited for; matrix products, arithmetic and copies ran while one was open for 13% of the time, Pallas kernels for 0%

profile of v1, /device:TPU:0, one launch (start us, length us, event | category | flops | bytes accessed | tf_op | source)
XLA Modules:
  0.0 326.5 jit_solution(17459196841000662712)
XLA Ops:
  8.7 8.4 %gather_fusion = s32[1536]{0:T(1024)S(1)} fusion(s32[1600]{0:T(1024)S(1)} %copy-done.1, s32[2048]{0:T(1024)S(1)} %pad_clamp_fusion), kind=kCustom, calls=%fused_computation | custom fusion | bytes 18432 | tf_op jit(solution)/shard_map/gather | solution.py:21
  17.2 1.2 reduce-window.6
  19.0 26.0 %all-gather.2.cloned.1.call-done = bf16[1536,1024]{1,0:T(8,128)(2,1)} async-done(((bf16[192,1024]{1,0:T(8,128)(2,1)}), bf16[1536,1024]{1,0:T(8,128)(2,1)}) %all-gather.2.cloned.1.call-update) | async-done | bytes 3145744 | tf_op jit(solution)/shard_map/all_gather | solution.py:62
  45.0 3.9 %convert_add_fusion = f32[1024,384]{1,0:T(8,128)S(1)} fusion(bf16[1536,1024]{1,0:T(8,128)(2,1)} %all-gather.2.cloned.1.call-done, bf16[1536,384]{1,0:T(8,128)(2,1)S(1)} %copy-done, bf16[1,1024,384]{2,1,0:T(8,128)(2,1)} %param.15), kind=kOutput, calls=%fused_computation.6 | convolution fusion | flops 1208745984 | bytes 6684672 | tf_op jit(solution)/shard_map/dot_general | solution.py:61
  48.9 2.2 fusion.45
  51.3 53.0 %all-reduce.5.cloned.1.call-done = f32[1024,32]{0,1:T(8,128)} async-done(((f32[1024,32]{0,1:T(8,128)}), f32[1024,32]{0,1:T(8,128)}) %all-reduce.5.cloned.1.call-update) | async-done | bytes 131088 | tf_op jit(solution)/shard_map/psum | solution.py:72
  104.3 6.8 %scatter_custom_fusion = s32[3072]{0:T(1024)} fusion(s32[1536]{0:T(1024)S(1)} %broadcast_select_fusion, s32[1536]{0:T(1024)S(1)} %get-tuple-element.13, s32[]{:T(128)} %constant.83.clone.1), kind=kCustom, calls=%fused_computation.70 | custom fusion | bytes 12292
  111.1 4.6 %all-to-all-start = ((s32[4,1,768]{2,1,0:T(1,128)}), s32[4,1,768]{2,1,0:T(1,128)S(1)}, u32[]{:S(2)}, u32[]{:S(2)}) async-start(s32[4,1,768]{2,1,0:T(1,128)} %bitcast.13), calls=%async_computation | async-start | bytes 24576 | tf_op jit(solution)/shard_map/all_to_all | solution.py:34
  115.7 5.7 %scatter_custom_fusion.1 = bf16[3072,128]{1,0:T(8,128)(2,1)} fusion(s32[1536]{0:T(1024)S(1)} %broadcast_select_fusion, bf16[1536,128]{1,0:T(8,128)(2,1)} %param.19, bf16[]{:T(256)} %constant.89.clone.1), kind=kCustom, calls=%fused_computation.11 | custom fusion | bytes 786944
  121.4 19.2 %all-reduce.7.cloned.1.call-done = f32[1024,32]{0,1:T(8,128)} async-done(((f32[1024,32]{0,1:T(8,128)}), f32[1024,32]{0,1:T(8,128)}) %all-reduce.7.cloned.1.call-update) | async-done | bytes 131088 | tf_op jit(solution)/shard_map/psum | solution.py:72
  140.6 1.2 fusion.15
  141.9 2.9 cholesky.44
  146.0 3.5 %all-to-all-start.1 = ((bf16[4,768,128]{2,1,0:T(8,128)(2,1)}), bf16[4,768,128]{2,1,0:T(8,128)(2,1)S(1)}, u32[]{:S(2)}, u32[]{:S(2)}) async-start(bf16[4,768,128]{2,1,0:T(8,128)(2,1)} %bitcast.15), calls=%async_computation.1 | async-start | bytes 1572864 | tf_op jit(solution)/shard_map/all_to_all | solution.py:33
  149.5 1.3 compare_reduce_fusion.1
  150.8 1.3 fusion.27
  152.1 3.2 custom-call.6
  155.2 1.2 fusion.9
  156.5 1.6 fusion.46
  158.1 21.1 %psum.44 = f32[384,32]{0,1:T(8,128)} all-reduce(f32[384,32]{0,1:T(8,128)} %fusion.46), channel_id=1, replica_groups=mesh['rep'=4,'tp'=8] {'rep'}, use_global_device_ids=true, to_apply=%region_4.0 | all-reduce | flops 12288 | bytes 98304 | tf_op jit(solution)/shard_map/psum | solution.py:78
  179.2 3.0 fusion.21
  182.5 51.0 %all-reduce.9.cloned.1.call-done = f32[1024,32]{0,1:T(8,128)} async-done(((f32[1024,32]{0,1:T(8,128)}), f32[1024,32]{0,1:T(8,128)}) %all-reduce.9.cloned.1.call-update) | async-done | bytes 131088 | tf_op jit(solution)/shard_map/psum | solution.py:72
  233.5 2.5 fusion.3
  236.0 33.6 %all-reduce.11.cloned.1.call-done = f32[1024,32]{0,1:T(8,128)} async-done(((f32[1024,32]{0,1:T(8,128)}), f32[1024,32]{0,1:T(8,128)}) %all-reduce.11.cloned.1.call-update) | async-done | bytes 131088 | tf_op jit(solution)/shard_map/psum | solution.py:72
  269.6 1.2 fusion.12
  270.9 2.9 cholesky.55
  275.2 2.4 custom-call.7
  277.6 1.2 fusion.7
  279.8 18.1 %psum.47 = f32[384,32]{0,1:T(8,128)S(1)} all-reduce(f32[384,32]{0,1:T(8,128)S(1)} %fusion.47), channel_id=1, replica_groups=mesh['rep'=4,'tp'=8] {'rep'}, use_global_device_ids=true, to_apply=%region_7.10 | all-reduce | flops 12288 | bytes 98304 | tf_op jit(solution)/shard_map/psum | solution.py:78
  298.0 1.5 fusion.48
  299.5 1.1 fusion.4
  300.6 1.0 fusion.44
  301.6 17.5 %all_gather.7 = bf16[1024,384]{1,0:T(8,128)(2,1)S(1)} all-gather(bf16[256,384]{1,0:T(8,128)(2,1)S(1)} %get-tuple-element.10), channel_id=1, replica_groups=mesh['rep'=4,'tp'=8] {'rep'}, dimensions={0}, use_global_device_ids=true | all-gather | bytes 983040 | tf_op jit(solution)/shard_map/all_gather | solution.py:87
  (57 shorter events, 7.2 us)
Async XLA Ops:
  7.2 37.8 %copy-start = (bf16[1536,384]{1,0:T(8,128)(2,1)S(1)}, bf16[1536,384]{1,0:T(8,128)(2,1)}, u32[]{:S(2)}) copy-start(bf16[1536,384]{1,0:T(8,128)(2,1)} %param.14) | copy-start | bytes 3538948
  7.2 1.5 copy-start.1
  7.2 37.8 %all-gather.2.cloned.1.call-start = ((), (), s32[]{:S(2)}) async-start(), calls=%async_computation.2 | async-start | bytes 3538944 | tf_op jit(solution)/shard_map/all_gather | solution.py:62
  7.9 96.4 %all-reduce.5.cloned.1.call-start = ((), (), s32[]{:S(2)}) async-start(), calls=%async_computation.3 | async-start | bytes 262144 | tf_op jit(solution)/shard_map/psum | solution.py:72
  8.7 10.2 %copy-start.9 = (s32[2]{0:T(128)S(1)}, s32[2]{0:T(128)}, u32[]{:S(2)}) copy-start(s32[2]{0:T(128)} %constant.95) | copy-start | bytes 28
  19.0 29.9 %copy-start.5 = (f32[384,32]{0,1:T(8,128)S(1)}, f32[384,32]{0,1:T(8,128)}, u32[]{:S(2)}) copy-start(f32[384,32]{0,1:T(8,128)} %param.16) | copy-start | bytes 147460
  48.9 2.3 copy-start.8
  51.2 89.4 %all-reduce.7.cloned.1.call-start = ((), (), s32[]{:S(2)}) async-start(), calls=%async_computation.4 | async-start | bytes 262144 | tf_op jit(solution)/shard_map/psum | solution.py:72
  111.1 34.3 %all-to-all-start = ((s32[4,1,768]{2,1,0:T(1,128)}), s32[4,1,768]{2,1,0:T(1,128)S(1)}, u32[]{:S(2)}, u32[]{:S(2)}) async-start(s32[4,1,768]{2,1,0:T(1,128)} %bitcast.13), calls=%async_computation | async-start | bytes 24576 | tf_op jit(solution)/shard_map/all_to_all | solution.py:34
  145.4 0.6 copy-start.6
  146.0 87.5 %all-to-all-start.1 = ((bf16[4,768,128]{2,1,0:T(8,128)(2,1)}), bf16[4,768,128]{2,1,0:T(8,128)(2,1)S(1)}, u32[]{:S(2)}, u32[]{:S(2)}) async-start(bf16[4,768,128]{2,1,0:T(8,128)(2,1)} %bitcast.15), calls=%async_computation.1 | async-start | bytes 1572864 | tf_op jit(solution)/shard_map/all_to_all | solution.py:33
  149.5 84.0 %all-reduce.9.cloned.1.call-start = ((), (), s32[]{:S(2)}) async-start(), calls=%async_computation.5 | async-start | bytes 262144 | tf_op jit(solution)/shard_map/psum | solution.py:72
  156.5 77.1 %copy-start.7 = (s32[4,1,768]{2,1,0:T(1,128)S(1)}, s32[4,1,768]{2,1,0:T(1,128)}, u32[]{:S(2)}) copy-start(s32[4,1,768]{2,1,0:T(1,128)} %copy-done.6) | copy-start | bytes 36868
  182.3 87.3 %all-reduce.11.cloned.1.call-start = ((), (), s32[]{:S(2)}) async-start(), calls=%async_computation.6 | async-start | bytes 262144 | tf_op jit(solution)/shard_map/psum | solution.py:72
  298.0 2.6 copy-start.4
  299.4 1.2 copy-start.2
  299.5 1.2 copy-start.3
Sparse Core Ops, SparseCore 0:
  9.9 35.0 all-gather.1
  51.3 52.9 all-reduce.4
  106.7 33.8 all-reduce.6
  182.4 51.0 all-reduce.8
  235.8 33.8 all-reduce.10
